TPU v7x, 128 devices: a whole 4x4x4 slice. The times are simulated.
128 devices in a mesh: lon: 32 (over z_lo, y, x), lat: 4 (over z_hi, core).
Axes of the slice: x: 4, y: 4, z: 4 (z_hi: 2, z_lo: 2; z = z_hi * 2 + z_lo), core: 2. Of those that a mesh axis runs over, the one named last changes fastest.
Arguments:
- increment: float32 [3, 8192, 1024], P(None, 'lon', 'lat'), may hold values from -6 to 6
- depth_field: float32 [8192, 1024], P('lon', 'lat'), may hold values from 0.5 to 1.5
- coriolis: float32 [1024], P('lat'), may hold values from -0.5 to 0.5
- footprint: bfloat16 [128, 128], replicated, may hold values from -0.5 to 0.5
- channel_weights: float32 [5, 3], replicated, may hold values from -3.5 to 3.5
- track_tiles: int32 [2, 4, 32, 32], P(None, 'lat', 'lon'), may hold values from -1 to 3, as said below
- innovations: bfloat16 [2, 4, 32, 32, 5, 128, 128], P(None, 'lat', 'lon'), may hold values from -6 to 6
- obs_weights: bfloat16 [2, 4, 32, 32], P(None, 'lat', 'lon'), may hold values from 0.25 to 2
Outputs:
- gradient: float32 [3, 8192, 1024], P(None, 'lon', 'lat')
Inputs may be any that keep to these rules, and one draw needn't show every extreme that they name: `track_tiles`: tiles are numbered 0 to 3 within a slab's block of a band. At every observation time, in every band, one owner observes a tile of every slab; other entries are -1 or a tile.
All inputs are finite; a program needn't handle non-finite values.
Results may differ from a plain program's by a relative error of at most 0.0028.
Values may be sent and summed in bfloat16 or wider, within the bound.
No kernel may reach another device: no remote copies, remote signals or barrier semaphores. Data moves between devices by JAX's collectives and lax.ppermute only.
A program may use at most 192 MiB of HBM per device.

v0:
```python
import jax
import jax.numpy as jnp
from jax import lax
from jax.sharding import PartitionSpec as P

TILE = 128
STEPS = 6
OBS_TIMES = 2


COURANT = 0.7


def extended(shard, sides, width, wrap):
    for axis, dim in sides:
        peers, length = (lax.axis_size(axis), shard.shape[dim])
        up = [(i, (i + 1) % peers) for i in range(peers if wrap else peers - 1)]
        down = [(j, i) for i, j in up]
        last = lax.slice_in_dim(shard, length - width, length, axis=dim)
        first = lax.slice_in_dim(shard, 0, width, axis=dim)
        before = lax.ppermute(last, axis, up)
        after = lax.ppermute(first, axis, down)
        shard = jnp.concatenate([before, shard, after], axis=dim)
    return shard


def lon_diff(padded):
    return 0.5 * (padded[2:, :] - padded[:-2, :])


def lat_diff(padded):
    return 0.5 * (padded[:, 2:] - padded[:, :-2])


def tl_lon(values):
    return extended(values, (("lon", 0),), 1, True)


def tl_lat(values):
    return extended(values, (("lat", 1),), 1, False)


def adj_lon(values):
    return extended(values, (("lon", 0),), 1, True)


def adj_lat(values):
    return extended(values, (("lat", 1),), 1, False)


def tangent_step(east_wind, north_wind, height, depth_field, coriolis):
    height_next = height - COURANT * (
        lon_diff(tl_lon(depth_field * east_wind)) + lat_diff(tl_lat(depth_field * north_wind))
    )
    east_next = east_wind + coriolis * north_wind - COURANT * lon_diff(tl_lon(height_next))
    north_next = north_wind - coriolis * east_next - COURANT * lat_diff(tl_lat(height_next))
    return (east_next, north_next, height_next)


def adjoint_step(east_adj, north_adj, height_adj, depth_field, coriolis):
    east_once = east_adj - coriolis * north_adj
    height_once = height_adj + COURANT * (
        lat_diff(adj_lat(north_adj)) + lon_diff(adj_lon(east_once))
    )
    east_prev = east_once + COURANT * depth_field * lon_diff(adj_lon(height_once))
    north_prev = (
        north_adj + coriolis * east_once + COURANT * depth_field * lat_diff(adj_lat(height_once))
    )
    return (east_prev, north_prev, height_once)


def to_tiles(block_data):
    fields, row_total, col_total = block_data.shape
    blocks = block_data.reshape(fields, row_total // TILE, TILE, col_total // TILE, TILE)
    return blocks.transpose(1, 3, 0, 2, 4).reshape(-1, fields, TILE, TILE)


def from_tiles(pieces, row_total, col_total):
    fields = pieces.shape[1]
    blocks = pieces.reshape(row_total // TILE, col_total // TILE, fields, TILE, TILE)
    return blocks.transpose(2, 0, 3, 1, 4).reshape(fields, row_total, col_total)


def residual_adjoint(arrived, innov, weights, footprint, channel_weights):
    highest = lax.Precision.HIGHEST
    spread = jnp.einsum("kcab,bd->kcad", arrived, footprint, preferred_element_type=jnp.float32)
    radiance = jnp.einsum("hc,kcad->khad", channel_weights, spread, precision=highest)
    weighted = weights.astype(jnp.float32)[:, None, None, None] * (
        radiance - innov.astype(jnp.float32)
    )
    back = jnp.einsum("hc,khad->kcad", channel_weights, weighted, precision=highest).astype(
        jnp.bfloat16
    )
    return jnp.einsum("kcad,bd->kcab", back, footprint, preferred_element_type=jnp.float32)


def observe(state, track_tiles, innovations, obs_weights, footprint, channel_weights, obs_index):
    stacked = jnp.stack(state)
    tiles = to_tiles(stacked).astype(jnp.bfloat16)
    track_row = track_tiles[obs_index, 0, 0]
    is_valid = track_row >= 0
    tile_index = jnp.maximum(track_row, 0)
    outgoing = jnp.take(tiles, tile_index, axis=0)
    innov_row = innovations[obs_index, 0, 0]
    weight_row = obs_weights[obs_index, 0, 0]
    arrived = lax.all_to_all(outgoing, "lon", split_axis=0, concat_axis=0, tiled=True)
    answer = residual_adjoint(arrived, innov_row, weight_row, footprint, channel_weights)
    returned = lax.all_to_all(answer, "lon", split_axis=0, concat_axis=0, tiled=True)
    numbers = jnp.arange(tiles.shape[0], dtype=jnp.int32)
    one_hot = ((tile_index[:, None] == numbers[None, :]) & is_valid[:, None]).astype(jnp.float32)
    forcing = jnp.einsum("ot,ocab->tcab", one_hot, returned, precision=lax.Precision.HIGHEST)
    return from_tiles(forcing, stacked.shape[1], stacked.shape[2])


def on_device(
    increment,
    depth_field,
    coriolis,
    footprint,
    channel_weights,
    track_tiles,
    innovations,
    obs_weights,
):
    interval = STEPS // OBS_TIMES
    east_wind, north_wind, height = (increment[0], increment[1], increment[2])
    forcings = []
    for step_index in range(STEPS):
        east_wind, north_wind, height = tangent_step(
            east_wind, north_wind, height, depth_field, coriolis
        )
        if (step_index + 1) % interval == 0:
            forcings.append(
                observe(
                    (east_wind, north_wind, height),
                    track_tiles,
                    innovations,
                    obs_weights,
                    footprint,
                    channel_weights,
                    (step_index + 1) // interval - 1,
                )
            )
    east_adj = jnp.zeros_like(depth_field)
    north_adj = jnp.zeros_like(depth_field)
    height_adj = jnp.zeros_like(depth_field)
    for step_index in range(STEPS, 0, -1):
        if step_index % interval == 0:
            forcing = forcings[step_index // interval - 1]
            east_adj = east_adj + forcing[0]
            north_adj = north_adj + forcing[1]
            height_adj = height_adj + forcing[2]
        east_adj, north_adj, height_adj = adjoint_step(
            east_adj, north_adj, height_adj, depth_field, coriolis
        )
    return increment + jnp.stack([east_adj, north_adj, height_adj])


def solution(mesh):
    return jax.shard_map(
        on_device,
        mesh=mesh,
        in_specs=(
            P(None, "lon", "lat"),
            P("lon", "lat"),
            P("lat"),
            P(),
            P(),
            P(None, "lat", "lon", None),
            P(None, "lat", "lon", None, None, None, None),
            P(None, "lat", "lon", None),
        ),
        out_specs=P(None, "lon", "lat"),
        check_vma=False,
    )
```

profile of v0, /device:TPU:1, one launch (start us, length us, event | category | flops | bytes accessed | tf_op | source)
XLA Modules:
  0.0 698.4 jit_solution(15582074501227702422)
XLA Ops:
  1.3 6.9 collective-permute-start.3
  24.0 7.0 collective-permute-start.7
  57.5 6.3 collective-permute-start.15
  89.3 6.3 collective-permute-start.23
  121.1 6.3 collective-permute-start.31
  147.1 5.9 collective-permute-start.36
  153.1 6.3 collective-permute-start.39
  184.9 6.3 collective-permute-start.47
  193.2 5.8 collective-permute-done.46
  211.6 12.7 %fusion.235 = (bf16[1,1,1,32,5,128,128]{6,5,4,3,2,1,0:T(8,128)(2,1)}, bf16[1,1,1,32,5,128,128]{6,5,4,3,2,1,0:T(8,128)(2,1)}) fusion(bf16[2,1,1,32,5,128,128]{6,5,4,3,2,1,0:T(8,128)(2,1)} %param.16), kind=kLoop, calls=%fused_computation.339 | loop fusion | bytes 20971520 | tf_op jit(solution)/shard_map/slice | solution.py:104
  231.9 17.0 %all-to-all-done = bf16[32,3,128,128]{3,2,1,0:T(8,128)(2,1)} async-done(((bf16[32,3,128,128]{3,2,1,0:T(8,128)(2,1)}), bf16[32,3,128,128]{3,2,1,0:T(8,128)(2,1)}, u32[]{:S(2)}, u32[]{:S(2)}) %all-to-all-start) | async-done | bytes 3145760 | tf_op jit(solution)/shard_map/all_to_all | solution.py:106
  257.1 23.0 %fusion.10 = f32[32,128,128,5]{2,3,1,0:T(8,128)} fusion(f32[32,3,128,128]{3,2,1,0:T(8,128)S(1)} %fusion.191, f32[5,3]{0,1:T(4,128)S(1)} %copy-done.4), kind=kOutput, calls=%fused_computation.14 | convolution fusion | flops 94371840 | bytes 16777276 | tf_op jit(solution)/shard_map/hc,kcad->khad/dot_general | solution.py:87
  280.0 32.9 %fusion.27 = bf16[32,3,128,128]{3,1,2,0:T(4,128)(2,1)S(1)} fusion(f32[32,128,128,5]{2,3,1,0:T(8,128)} %fusion.10, bf16[1,1,1,32,5,128,128]{6,5,4,3,2,1,0:T(8,128)(2,1)S(1)} %bitcast.169, f32[32]{0:T(128)S(1)} %get-tuple-element.162, f32[5,3]{0,1:T(4,128)S(1)} %copy-done.4), kind=kOutput, calls=%fused_computation.25 | convolution fusion | flops 103809024 | bytes 18874556 | tf_op jit(solution)/shard_map/hc,khad->kcad/dot_general | solution.py:91
  316.4 8.2 %all-to-all-start.1 = ((f32[32,3,128,128]{3,2,1,0:T(8,128)}), f32[32,3,128,128]{3,2,1,0:T(8,128)}, u32[]{:S(2)}, u32[]{:S(2)}) async-start(f32[32,3,128,128]{3,2,1,0:T(8,128)} %fusion.32), calls=%async_computation.1 | async-start | bytes 12582912 | tf_op jit(solution)/shard_map/all_to_all | solution.py:108
  325.6 23.0 %fusion.8 = f32[32,128,128,5]{2,3,1,0:T(8,128)} fusion(f32[32,3,128,128]{3,2,1,0:T(8,128)S(1)} %fusion.188, f32[5,3]{0,1:T(4,128)S(1)} %copy-done.4), kind=kOutput, calls=%fused_computation.12 | convolution fusion | flops 94371840 | bytes 16777276 | tf_op jit(solution)/shard_map/hc,kcad->khad/dot_general | solution.py:87
  348.6 33.1 %fusion.24 = bf16[32,3,128,128]{3,1,2,0:T(4,128)(2,1)S(1)} fusion(f32[32,128,128,5]{2,3,1,0:T(8,128)} %fusion.8, bf16[1,1,1,32,5,128,128]{6,5,4,3,2,1,0:T(8,128)(2,1)S(1)} %bitcast.167, f32[32]{0:T(128)S(1)} %get-tuple-element.161, f32[5,3]{0,1:T(4,128)S(1)} %copy-done.4), kind=kOutput, calls=%fused_computation.24 | convolution fusion | flops 103809024 | bytes 18874556 | tf_op jit(solution)/shard_map/hc,khad->kcad/dot_general | solution.py:91
  385.3 20.1 %all-to-all-done.1 = f32[32,3,128,128]{3,2,1,0:T(8,128)} async-done(((f32[32,3,128,128]{3,2,1,0:T(8,128)}), f32[32,3,128,128]{3,2,1,0:T(8,128)}, u32[]{:S(2)}, u32[]{:S(2)}) %all-to-all-start.1) | async-done | bytes 6291488 | tf_op jit(solution)/shard_map/all_to_all | solution.py:108
  405.5 7.7 %all-to-all-start.3 = ((f32[32,3,128,128]{3,2,1,0:T(8,128)}), f32[32,3,128,128]{3,2,1,0:T(8,128)}, u32[]{:S(2)}, u32[]{:S(2)}) async-start(f32[32,3,128,128]{3,2,1,0:T(8,128)} %fusion.30), calls=%async_computation.3 | async-start | bytes 12582912 | tf_op jit(solution)/shard_map/all_to_all | solution.py:108
  413.2 8.1 %fusion.16 = f32[4,3,128,128]{3,0,2,1:T(4,128)S(1)} fusion(f32[32,3,128,128]{3,2,1,0:T(8,128)} %all-to-all-done.1, s32[32]{0:T(128)S(1)} %get-tuple-element.158, pred[32]{0:T(512)(128)(4,1)S(1)} %get-tuple-element.156), kind=kOutput, calls=%fused_computation.20 | convolution fusion | flops 75497728 | bytes 7078048 | tf_op jit(solution)/shard_map/ot,ocab->tcab/dot_general | solution.py:111
  432.2 72.8 %collective-permute-done.51 = f32[1,256]{1,0:T(1,128)S(1)} collective-permute-done((f32[1,256]{1,0:T(1,128)S(1)}, f32[1,256]{1,0:T(1,128)S(1)}, u32[]{:S(2)}, u32[]{:S(2)}) %collective-permute-start.51) | collective-permute-done | bytes 1056 | tf_op jit(solution)/shard_map/ppermute | solution.py:21
  505.0 7.0 collective-permute-done.50
  538.4 5.8 collective-permute-done.56
  571.1 8.1 %fusion.14 = f32[4,3,128,128]{3,0,2,1:T(4,128)S(1)} fusion(f32[32,3,128,128]{3,2,1,0:T(8,128)} %all-to-all-done.3, s32[32]{0:T(128)S(1)} %get-tuple-element.157, pred[32]{0:T(512)(128)(4,1)S(1)} %get-tuple-element.155), kind=kOutput, calls=%fused_computation.18 | convolution fusion | flops 75497728 | bytes 7078048 | tf_op jit(solution)/shard_map/ot,ocab->tcab/dot_general | solution.py:111
  648.1 5.9 collective-permute-start.84
  (321 shorter events, 353.7 us)
Async XLA Ops:
  1.3 14.6 %collective-permute-start.3 = (f32[256,1]{1,0:T(8,128)S(1)}, f32[256,1]{1,0:T(8,128)S(1)}, u32[]{:S(2)}, u32[]{:S(2)}) collective-permute-start(f32[256,1]{1,0:T(8,128)S(1)} %get-tuple-element.154), channel_id=1, source_target_pairs={{0,1},{1,2},{2,3},{4,5},{5,6},{6,7},{8,9},{9,10},{10,11},{12,13},{... | collective-permute-start | bytes 3080 | tf_op jit(solution)/shard_map/ppermute | solution.py:21
  18.1 14.8 %collective-permute-start.5 = (f32[1,256]{1,0:T(1,128)S(1)}, f32[1,256]{1,0:T(1,128)S(1)}, u32[]{:S(2)}, u32[]{:S(2)}) collective-permute-start(f32[1,256]{1,0:T(1,128)S(1)} %get-tuple-element.148), channel_id=1, source_target_pairs={{0,4},{4,8},{8,12},{12,16},{16,20},{20,24},{24,28},{28,32},{32,36}... | collective-permute-start | bytes 3080 | tf_op jit(solution)/shard_map/ppermute | solution.py:21
  18.5 14.4 %collective-permute-start.4 = (f32[1,256]{1,0:T(1,128)S(1)}, f32[1,256]{1,0:T(1,128)S(1)}, u32[]{:S(2)}, u32[]{:S(2)}) collective-permute-start(f32[1,256]{1,0:T(1,128)S(1)} %get-tuple-element.147), channel_id=1, source_target_pairs={{4,0},{8,4},{12,8},{16,12},{20,16},{24,20},{28,24},{32,28},{36,32}... | collective-permute-start | bytes 3080 | tf_op jit(solution)/shard_map/ppermute | solution.py:22
  51.6 14.1 %collective-permute-start.13 = (f32[1,256]{1,0:T(1,128)S(1)}, f32[1,256]{1,0:T(1,128)S(1)}, u32[]{:S(2)}, u32[]{:S(2)}) collective-permute-start(f32[1,256]{1,0:T(1,128)S(1)} %get-tuple-element.140), channel_id=1, source_target_pairs={{0,4},{4,8},{8,12},{12,16},{16,20},{20,24},{24,28},{28,32},{32,36}... | collective-permute-start | bytes 3080 | tf_op jit(solution)/shard_map/ppermute | solution.py:21
  51.7 14.0 %collective-permute-start.12 = (f32[1,256]{1,0:T(1,128)S(1)}, f32[1,256]{1,0:T(1,128)S(1)}, u32[]{:S(2)}, u32[]{:S(2)}) collective-permute-start(f32[1,256]{1,0:T(1,128)S(1)} %get-tuple-element.139), channel_id=1, source_target_pairs={{4,0},{8,4},{12,8},{16,12},{20,16},{24,20},{28,24},{32,28},{36,32}... | collective-permute-start | bytes 3080 | tf_op jit(solution)/shard_map/ppermute | solution.py:22
  83.4 14.1 %collective-permute-start.21 = (f32[1,256]{1,0:T(1,128)S(1)}, f32[1,256]{1,0:T(1,128)S(1)}, u32[]{:S(2)}, u32[]{:S(2)}) collective-permute-start(f32[1,256]{1,0:T(1,128)S(1)} %get-tuple-element.132), channel_id=1, source_target_pairs={{0,4},{4,8},{8,12},{12,16},{16,20},{20,24},{24,28},{28,32},{32,36}... | collective-permute-start | bytes 3080 | tf_op jit(solution)/shard_map/ppermute | solution.py:21
  83.5 14.0 %collective-permute-start.20 = (f32[1,256]{1,0:T(1,128)S(1)}, f32[1,256]{1,0:T(1,128)S(1)}, u32[]{:S(2)}, u32[]{:S(2)}) collective-permute-start(f32[1,256]{1,0:T(1,128)S(1)} %get-tuple-element.131), channel_id=1, source_target_pairs={{4,0},{8,4},{12,8},{16,12},{20,16},{24,20},{28,24},{32,28},{36,32}... | collective-permute-start | bytes 3080 | tf_op jit(solution)/shard_map/ppermute | solution.py:22
  115.3 14.1 %collective-permute-start.29 = (f32[1,256]{1,0:T(1,128)S(1)}, f32[1,256]{1,0:T(1,128)S(1)}, u32[]{:S(2)}, u32[]{:S(2)}) collective-permute-start(f32[1,256]{1,0:T(1,128)S(1)} %get-tuple-element.123), channel_id=1, source_target_pairs={{0,4},{4,8},{8,12},{12,16},{16,20},{20,24},{24,28},{28,32},{32,36}... | collective-permute-start | bytes 3080 | tf_op jit(solution)/shard_map/ppermute | solution.py:21
  115.3 14.0 %collective-permute-start.28 = (f32[1,256]{1,0:T(1,128)S(1)}, f32[1,256]{1,0:T(1,128)S(1)}, u32[]{:S(2)}, u32[]{:S(2)}) collective-permute-start(f32[1,256]{1,0:T(1,128)S(1)} %get-tuple-element.122), channel_id=1, source_target_pairs={{4,0},{8,4},{12,8},{16,12},{20,16},{24,20},{28,24},{32,28},{36,32}... | collective-permute-start | bytes 3080 | tf_op jit(solution)/shard_map/ppermute | solution.py:22
  147.0 14.3 %collective-permute-start.37 = (f32[1,256]{1,0:T(1,128)S(1)}, f32[1,256]{1,0:T(1,128)S(1)}, u32[]{:S(2)}, u32[]{:S(2)}) collective-permute-start(f32[1,256]{1,0:T(1,128)S(1)} %get-tuple-element.115), channel_id=1, source_target_pairs={{0,4},{4,8},{8,12},{12,16},{16,20},{20,24},{24,28},{28,32},{32,36}... | collective-permute-start | bytes 3080 | tf_op jit(solution)/shard_map/ppermute | solution.py:21
  147.1 14.2 %collective-permute-start.36 = (f32[1,256]{1,0:T(1,128)S(1)}, f32[1,256]{1,0:T(1,128)S(1)}, u32[]{:S(2)}, u32[]{:S(2)}) collective-permute-start(f32[1,256]{1,0:T(1,128)S(1)} %get-tuple-element.114), channel_id=1, source_target_pairs={{4,0},{8,4},{12,8},{16,12},{20,16},{24,20},{28,24},{32,28},{36,32}... | collective-permute-start | bytes 3080 | tf_op jit(solution)/shard_map/ppermute | solution.py:22
  179.1 14.0 %collective-permute-start.45 = (f32[1,256]{1,0:T(1,128)S(1)}, f32[1,256]{1,0:T(1,128)S(1)}, u32[]{:S(2)}, u32[]{:S(2)}) collective-permute-start(f32[1,256]{1,0:T(1,128)S(1)} %get-tuple-element.107), channel_id=1, source_target_pairs={{0,4},{4,8},{8,12},{12,16},{16,20},{20,24},{24,28},{28,32},{32,36}... | collective-permute-start | bytes 3080 | tf_op jit(solution)/shard_map/ppermute | solution.py:21
  179.2 14.0 %collective-permute-start.44 = (f32[1,256]{1,0:T(1,128)S(1)}, f32[1,256]{1,0:T(1,128)S(1)}, u32[]{:S(2)}, u32[]{:S(2)}) collective-permute-start(f32[1,256]{1,0:T(1,128)S(1)} %get-tuple-element.106), channel_id=1, source_target_pairs={{4,0},{8,4},{12,8},{16,12},{20,16},{24,20},{28,24},{32,28},{36,32}... | collective-permute-start | bytes 3080 | tf_op jit(solution)/shard_map/ppermute | solution.py:22
  206.8 42.1 %all-to-all-start = ((bf16[32,3,128,128]{3,2,1,0:T(8,128)(2,1)}), bf16[32,3,128,128]{3,2,1,0:T(8,128)(2,1)}, u32[]{:S(2)}, u32[]{:S(2)}) async-start(bf16[32,3,128,128]{3,2,1,0:T(8,128)(2,1)} %broadcast_select_fusion.1), calls=%async_computation | async-start | bytes 6291456 | tf_op jit(solution)/shard_map/all_to_all | solution.py:106
  248.9 67.5 %all-to-all-start.2 = ((bf16[32,3,128,128]{3,2,1,0:T(8,128)(2,1)}), bf16[32,3,128,128]{3,2,1,0:T(8,128)(2,1)S(1)}, u32[]{:S(2)}, u32[]{:S(2)}) async-start(bf16[32,3,128,128]{3,2,1,0:T(8,128)(2,1)} %broadcast_select_fusion), calls=%async_computation.2 | async-start | bytes 6291456 | tf_op jit(solution)/shard_map/all_to_all | solution.py:106
  316.4 89.0 %all-to-all-start.1 = ((f32[32,3,128,128]{3,2,1,0:T(8,128)}), f32[32,3,128,128]{3,2,1,0:T(8,128)}, u32[]{:S(2)}, u32[]{:S(2)}) async-start(f32[32,3,128,128]{3,2,1,0:T(8,128)} %fusion.32), calls=%async_computation.1 | async-start | bytes 12582912 | tf_op jit(solution)/shard_map/all_to_all | solution.py:108
  405.5 165.6 %all-to-all-start.3 = ((f32[32,3,128,128]{3,2,1,0:T(8,128)}), f32[32,3,128,128]{3,2,1,0:T(8,128)}, u32[]{:S(2)}, u32[]{:S(2)}) async-start(f32[32,3,128,128]{3,2,1,0:T(8,128)} %fusion.30), calls=%async_computation.3 | async-start | bytes 12582912 | tf_op jit(solution)/shard_map/all_to_all | solution.py:108
  421.8 83.2 %collective-permute-start.51 = (f32[1,256]{1,0:T(1,128)S(1)}, f32[1,256]{1,0:T(1,128)S(1)}, u32[]{:S(2)}, u32[]{:S(2)}) collective-permute-start(f32[1,256]{1,0:T(1,128)S(1)} %get-tuple-element.105), channel_id=1, source_target_pairs={{0,4},{4,8},{8,12},{12,16},{16,20},{20,24},{24,28},{28,32},{32,36}... | collective-permute-start | bytes 3080 | tf_op jit(solution)/shard_map/ppermute | solution.py:21
  423.3 88.7 %collective-permute-start.50 = (f32[1,256]{1,0:T(1,128)S(1)}, f32[1,256]{1,0:T(1,128)S(1)}, u32[]{:S(2)}, u32[]{:S(2)}) collective-permute-start(f32[1,256]{1,0:T(1,128)S(1)} %get-tuple-element.104), channel_id=1, source_target_pairs={{4,0},{8,4},{12,8},{16,12},{20,16},{24,20},{28,24},{32,28},{36,32}... | collective-permute-start | bytes 3080 | tf_op jit(solution)/shard_map/ppermute | solution.py:22
  427.7 84.2 %collective-permute-start.49 = (f32[256,1]{1,0:T(8,128)S(1)}, f32[256,1]{1,0:T(8,128)S(1)}, u32[]{:S(2)}, u32[]{:S(2)}) collective-permute-start(f32[256,1]{1,0:T(8,128)S(1)} %get-tuple-element.103), channel_id=1, source_target_pairs={{0,1},{1,2},{2,3},{4,5},{5,6},{6,7},{8,9},{9,10},{10,11},{12,13},{... | collective-permute-start | bytes 3080 | tf_op jit(solution)/shard_map/ppermute | solution.py:21
  429.7 82.3 %collective-permute-start.48 = (f32[256,1]{1,0:T(8,128)S(1)}, f32[256,1]{1,0:T(8,128)S(1)}, u32[]{:S(2)}, u32[]{:S(2)}) collective-permute-start(f32[256,1]{1,0:T(8,128)S(1)} %get-tuple-element.102), channel_id=1, source_target_pairs={{1,0},{2,1},{3,2},{5,4},{6,5},{7,6},{9,8},{10,9},{11,10},{13,12},{... | collective-permute-start | bytes 3080 | tf_op jit(solution)/shard_map/ppermute | solution.py:22
  560.7 18.5 %collective-permute-start.67 = (f32[1,256]{1,0:T(1,128)S(1)}, f32[1,256]{1,0:T(1,128)S(1)}, u32[]{:S(2)}, u32[]{:S(2)}) collective-permute-start(f32[1,256]{1,0:T(1,128)S(1)} %get-tuple-element.89), channel_id=1, source_target_pairs={{0,4},{4,8},{8,12},{12,16},{16,20},{20,24},{24,28},{28,32},{32,36}... | collective-permute-start | bytes 3080 | tf_op jit(solution)/shard_map/ppermute | solution.py:21
  560.8 18.5 %collective-permute-start.66 = (f32[1,256]{1,0:T(1,128)S(1)}, f32[1,256]{1,0:T(1,128)S(1)}, u32[]{:S(2)}, u32[]{:S(2)}) collective-permute-start(f32[1,256]{1,0:T(1,128)S(1)} %get-tuple-element.88), channel_id=1, source_target_pairs={{4,0},{8,4},{12,8},{16,12},{20,16},{24,20},{28,24},{32,28},{36,32}... | collective-permute-start | bytes 3080 | tf_op jit(solution)/shard_map/ppermute | solution.py:22
  579.6 13.8 %collective-permute-start.69 = (f32[1,256]{1,0:T(1,128)S(1)}, f32[1,256]{1,0:T(1,128)S(1)}, u32[]{:S(2)}, u32[]{:S(2)}) collective-permute-start(f32[1,256]{1,0:T(1,128)S(1)} %get-tuple-element.85), channel_id=1, source_target_pairs={{0,4},{4,8},{8,12},{12,16},{16,20},{20,24},{24,28},{28,32},{32,36}... | collective-permute-start | bytes 3080 | tf_op jit(solution)/shard_map/ppermute | solution.py:21
  (87 other events, 1295.6 us)
where the time goes:
time: 709 us; the launch traced here: 698 us
  starting transfers between devices  300 us (42%)
  waiting for transfers between devices  214 us (30%)
  matrix products  139 us (20%)
  local copies, waits for them, and re-layouts  22 us (3%)
  other arithmetic  21.3 us (3%)
    ppermute x48, starting transfers between devices, extended(): after = lax.ppermute(first, axis, down)  184 us
    ppermute x48, waiting for transfers between devices, extended(): after = lax.ppermute(first, axis, down)  97.1 us
    ppermute x48, starting transfers between devices, extended(): before = lax.ppermute(last, axis, up)  90.2 us
    ppermute x48, waiting for transfers between devices, extended(): before = lax.ppermute(last, axis, up)  79.2 us
    dot_general x2, matrix products, residual_adjoint(): jnp.einsum('hc,khad->kcad', channel_weights, weighted, precision=highest)  65.9 us
    dot_general x2, matrix products, residual_adjoint(): jnp.einsum('hc,kcad->khad', channel_weights, spread, precision=highest)  45.9 us
    all_to_all x2, waiting for transfers between devices, observe(): lax.all_to_all(answer, 'lon', split_axis=0, concat_axis=0, tiled=True)  20.1 us
    all_to_all x2, waiting for transfers between devices, observe(): lax.all_to_all(outgoing, 'lon', split_axis=0, concat_axis=0, tiled=True)  17 us
  transfers between devices with their start and end apart: 100, of which 27 were waited for; matrix products, arithmetic and copies ran while one was open for 24% of the time, Pallas kernels for 0%

commit v1 on v0

v1 whole, which is shorter than its diff:
```python
import jax
import jax.numpy as jnp
from jax import lax
from jax.sharding import PartitionSpec as P

TILE = 128
STEPS = 6
OBS_TIMES = 2
HALO = 2 * STEPS


COURANT = 0.7


def extend_lon(x, width):
    peers, length = lax.axis_size("lon"), x.shape[-2]
    up = [(i, (i + 1) % peers) for i in range(peers)]
    down = [(j, i) for i, j in up]
    before = lax.ppermute(x[..., length - width :, :], "lon", up)
    after = lax.ppermute(x[..., :width, :], "lon", down)
    return jnp.concatenate([before, x, after], axis=-2)


def extend_lat(x, width):
    peers, length = lax.axis_size("lat"), x.shape[-1]
    up = [(i, i + 1) for i in range(peers - 1)]
    down = [(j, i) for i, j in up]
    before = lax.ppermute(x[..., length - width :], "lat", up)
    after = lax.ppermute(x[..., :width], "lat", down)
    return jnp.concatenate([before, x, after], axis=-1)


def extend(x, width):
    return extend_lat(extend_lon(x, width), width)


def lon_diff(values):
    return 0.5 * (jnp.roll(values, -1, axis=0) - jnp.roll(values, 1, axis=0))


def lat_diff(values):
    return 0.5 * (jnp.roll(values, -1, axis=1) - jnp.roll(values, 1, axis=1))


def tangent_step(east_wind, north_wind, height, depth_field, coriolis, inside):
    height_next = height - COURANT * (
        lon_diff(depth_field * east_wind) + lat_diff(depth_field * north_wind)
    )
    height_next = jnp.where(inside, height_next, 0.0)
    east_next = east_wind + coriolis * north_wind - COURANT * lon_diff(height_next)
    north_next = north_wind - coriolis * east_next - COURANT * lat_diff(height_next)
    north_next = jnp.where(inside, north_next, 0.0)
    return (east_next, north_next, height_next)


def adjoint_step(east_adj, north_adj, height_adj, depth_field, coriolis, inside):
    east_once = east_adj - coriolis * north_adj
    height_once = height_adj + COURANT * (lat_diff(north_adj) + lon_diff(east_once))
    height_once = jnp.where(inside, height_once, 0.0)
    east_prev = east_once + COURANT * depth_field * lon_diff(height_once)
    north_prev = north_adj + coriolis * east_once + COURANT * depth_field * lat_diff(height_once)
    north_prev = jnp.where(inside, north_prev, 0.0)
    return (east_prev, north_prev, height_once)


def to_tiles(block_data):
    fields, row_total, col_total = block_data.shape
    blocks = block_data.reshape(fields, row_total // TILE, TILE, col_total // TILE, TILE)
    return blocks.transpose(1, 3, 0, 2, 4).reshape(-1, fields, TILE, TILE)


def from_tiles(pieces, row_total, col_total):
    fields = pieces.shape[1]
    blocks = pieces.reshape(row_total // TILE, col_total // TILE, fields, TILE, TILE)
    return blocks.transpose(2, 0, 3, 1, 4).reshape(fields, row_total, col_total)


def observe(state, track_row, innov_row, weight_row, footprint, channel_weights):
    highest = lax.Precision.HIGHEST
    tiles = to_tiles(state).astype(jnp.bfloat16)
    spread = jnp.einsum("jcab,bd->jcad", tiles, footprint, preferred_element_type=jnp.float32)
    radiance = jnp.einsum("hc,jcad->jhad", channel_weights, spread, precision=highest)
    is_valid = track_row >= 0
    tile_index = jnp.maximum(track_row, 0)
    chosen = jnp.take(radiance, tile_index, axis=0)
    weighted = weight_row.astype(jnp.float32)[:, None, None, None] * (
        chosen - innov_row.astype(jnp.float32)
    )
    back = jnp.einsum("hc,ohad->ocad", channel_weights, weighted, precision=highest).astype(
        jnp.bfloat16
    )
    numbers = jnp.arange(tiles.shape[0], dtype=jnp.int32)
    one_hot = ((tile_index[:, None] == numbers[None, :]) & is_valid[:, None]).astype(jnp.float32)
    summed = jnp.einsum("ot,ocad->tcad", one_hot, back.astype(jnp.float32), precision=highest)
    forcing = jnp.einsum(
        "tcad,bd->tcab", summed, footprint.astype(jnp.float32), precision=highest
    )
    return from_tiles(forcing, state.shape[1], state.shape[2])


def on_device(
    increment,
    depth_field,
    coriolis,
    footprint,
    channel_weights,
    track_tiles,
    innovations,
    obs_weights,
):
    interval = STEPS // OBS_TIMES
    rows, cols = depth_field.shape
    band = lax.axis_index("lat")
    lat_total = cols * lax.axis_size("lat")

    innov = innovations[:, 0, 0]
    innov = lax.all_to_all(innov, "lon", split_axis=1, concat_axis=1, tiled=True)
    weights = obs_weights[:, 0, 0]
    weights = lax.all_to_all(weights, "lon", split_axis=1, concat_axis=1, tiled=True)
    tracks = track_tiles[:, 0, 0]

    lat_global = band * cols - HALO + jnp.arange(cols + 2 * HALO, dtype=jnp.int32)
    inside = ((lat_global >= 0) & (lat_global < lat_total))[None, :]
    cor = extend_lat(coriolis[None, :], HALO)

    fields = extend(jnp.concatenate([increment, depth_field[None]], axis=0), HALO)
    east_wind, north_wind, height, depth = fields[0], fields[1], fields[2], fields[3]
    inner = (slice(HALO, HALO + rows), slice(HALO, HALO + cols))

    forcings = []
    for step_index in range(STEPS):
        east_wind, north_wind, height = tangent_step(
            east_wind, north_wind, height, depth, cor, inside
        )
        if (step_index + 1) % interval == 0:
            obs_index = (step_index + 1) // interval - 1
            state = jnp.stack([east_wind[inner], north_wind[inner], height[inner]])
            forcing = observe(
                state,
                tracks[obs_index],
                innov[obs_index],
                weights[obs_index],
                footprint,
                channel_weights,
            )
            forcings.append(extend(forcing, HALO))

    east_adj = jnp.zeros_like(depth)
    north_adj = jnp.zeros_like(depth)
    height_adj = jnp.zeros_like(depth)
    for step_index in range(STEPS, 0, -1):
        if step_index % interval == 0:
            forcing = forcings[step_index // interval - 1]
            east_adj = east_adj + forcing[0]
            north_adj = north_adj + forcing[1]
            height_adj = height_adj + forcing[2]
        east_adj, north_adj, height_adj = adjoint_step(
            east_adj, north_adj, height_adj, depth, cor, inside
        )
    adjoint = jnp.stack([east_adj[inner], north_adj[inner], height_adj[inner]])
    return increment + adjoint


def solution(mesh):
    return jax.shard_map(
        on_device,
        mesh=mesh,
        in_specs=(
            P(None, "lon", "lat"),
            P("lon", "lat"),
            P("lat"),
            P(),
            P(),
            P(None, "lat", "lon", None),
            P(None, "lat", "lon", None, None, None, None),
            P(None, "lat", "lon", None),
        ),
        out_specs=P(None, "lon", "lat"),
        check_vma=False,
    )
```

time: 709 us -> 350 us (0.49)
  starting transfers between devices: 300 us -> 69.5 us
  waiting for transfers between devices: 214 us -> 120 us
  matrix products: 139 us -> 67.5 us
  local copies, waits for them, and re-layouts: 22 us -> 46.8 us
  other arithmetic: 21.3 us -> 38.7 us
    ppermute x96 -> x14, starting transfers between devices: 274 us -> 54.4 us  [the longest x4 20.1 us: extend_lat(): before = lax.ppermute(x[..., length - width:], 'lat', up)]
    ppermute x96 -> x14, waiting for transfers between devices: 176 us -> 5.87 us  [the longest x3 4.69 us: extend_lon(): before = lax.ppermute(x[..., length - width:, :], 'lon', up)]
    all_to_all x4 -> x2, waiting for transfers between devices: 37.2 us -> 115 us  [the longest x1 115 us: on_device(): lax.all_to_all(innov, 'lon', split_axis=1, concat_axis=1, tiled=True)]
    dot_general x10, matrix products: 139 us -> 67.5 us  [the longest x2 54.4 us: observe(): jnp.einsum('hc,ohad->ocad', channel_weights, weighted, precision=highest)]
    unnamed x23 -> x17, local copies, waits for them, and re-layouts: 0.07 us -> 15.7 us
    mul x0 -> x1, other arithmetic: none -> 15.5 us  [observe(): weight_row.astype(jnp.float32)[:, None, None, None]]
    all_to_all x4 -> x2, starting transfers between devices: 25.7 us -> 15.1 us  [the longest x1 8.06 us: on_device(): lax.all_to_all(innov, 'lon', split_axis=1, concat_axis=1, tiled=True)]
    slice x57 -> x107, local copies, waits for them, and re-layouts: 16.1 us -> 13 us  [the longest x48 8.31 us: lon_diff(): return 0.5 * (jnp.roll(values, -1, axis=0) - jnp.roll(values, 1, axis=0))]
  transfers between devices with their start and end apart: 100 -> 16, of which waited for: 27 -> 3; matrix products, arithmetic and copies ran while one was open for 24% -> 26% of each run, Pallas kernels for 0% -> 0%
where the time goes in v1:
time: 350 us; the launch traced here: 344 us
  waiting for transfers between devices  120 us (34%)
  starting transfers between devices  69.5 us (20%)
  matrix products  67.5 us (19%)
  local copies, waits for them, and re-layouts  46.8 us (13%)
  other arithmetic  38.7 us (11%)
    all_to_all x1, waiting for transfers between devices, on_device(): lax.all_to_all(innov, 'lon', split_axis=1, concat_axis=1, tiled=True)  115 us
    dot_general x2, matrix products, observe(): jnp.einsum('hc,ohad->ocad', channel_weights, weighted, precision=highest)  54.4 us
    ppermute x4, starting transfers between devices, extend_lat(): before = lax.ppermute(x[..., length - width:], 'lat', up)  20.1 us
    ppermute x3, starting transfers between devices, extend_lon(): after = lax.ppermute(x[..., :width, :], 'lon', down)  17.8 us
    unnamed x17, local copies, waits for them, and re-layouts  15.7 us
    mul x1, other arithmetic, observe(): weight_row.astype(jnp.float32)[:, None, None, None]  15.5 us
    gather x2, local copies, waits for them, and re-layouts, observe(): chosen = jnp.take(radiance, tile_index, axis=0)  10.3 us
    ppermute x4, starting transfers between devices, extend_lat(): after = lax.ppermute(x[..., :width], 'lat', down)  9.1 us
  transfers between devices with their start and end apart: 16, of which 3 were waited for; matrix products, arithmetic and copies ran while one was open for 26% of the time, Pallas kernels for 0%

profile of v1, /device:TPU:1, one launch (start us, length us, event | category | flops | bytes accessed | tf_op | source)
XLA Modules:
  0.0 344.4 jit_solution(11804029655060533845)
XLA Ops:
  4.6 7.1 %collective-permute-start.1 = (f32[4,12,256]{1,0,2:T(4,128)}, f32[4,12,256]{1,0,2:T(4,128)S(1)}, u32[]{:S(2)}, u32[]{:S(2)}) collective-permute-start(f32[4,12,256]{1,0,2:T(4,128)} %get-tuple-element.50), channel_id=1, source_target_pairs={{4,0},{8,4},{12,8},{16,12},{20,16},{24,20},{28,24},{32,28},{36,32}... | collective-permute-start | bytes 147464 | tf_op jit(solution)/shard_map/ppermute | solution.py:20
  11.8 2.9 collective-permute-start.5
  14.6 5.1 %collective-permute-start.4 = (f32[1,12]{1,0:T(1,128)S(1)}, f32[1,12]{1,0:T(1,128)S(1)}, u32[]{:S(2)}, u32[]{:S(2)}) collective-permute-start(f32[1,12]{1,0:T(1,128)S(1)} %get-tuple-element.258), channel_id=1, source_target_pairs={{0,1},{1,2},{2,3},{4,5},{5,6},{6,7},{8,9},{9,10},{10,11},{12,13},{... | collective-permute-start | bytes 152 | tf_op jit(solution)/shard_map/ppermute | solution.py:28
  20.4 7.0 %all-to-all-start = ((bf16[2,32,1]{0,2,1:T(2,128)(2,1)}), bf16[2,32,1]{0,2,1:T(2,128)(2,1)S(1)}, u32[]{:S(2)}, u32[]{:S(2)}) async-start(bf16[2,32,1]{0,2,1:T(2,128)(2,1)} %copy.58), calls=%async_computation | async-start | bytes 32768 | tf_op jit(solution)/shard_map/all_to_all | solution.py:119
  28.7 12.7 %copy.187 = bf16[2,1,1,32,5,128,128]{6,5,4,0,3,2,1:T(8,128)(2,1)} copy(bf16[2,1,1,32,5,128,128]{6,5,4,3,2,1,0:T(8,128)(2,1)} %param.16) | data formatting | bytes 20971520 | tf_op args[6]
  43.9 5.1 %collective-permute-start.2 = (f32[4,280,12]{1,0,2:T(4,128)S(1)}, f32[4,280,12]{1,0,2:T(4,128)S(1)}, u32[]{:S(2)}, u32[]{:S(2)}) collective-permute-start(f32[4,280,12]{1,0,2:T(4,128)S(1)} %get-tuple-element.39), channel_id=1, source_target_pairs={{0,1},{1,2},{2,3},{4,5},{5,6},{6,7},{8,9},{9,10},{10,11},{12,13},{... | collective-permute-start | bytes 161288 | tf_op jit(solution)/shard_map/ppermute | solution.py:28
  49.0 8.1 %all-to-all-start.1 = ((bf16[2,32,5,128,128]{4,3,2,0,1:T(8,128)(2,1)}), bf16[2,32,5,128,128]{4,3,2,0,1:T(8,128)(2,1)}, u32[]{:S(2)}, u32[]{:S(2)}) async-start(bf16[2,32,5,128,128]{4,3,2,0,1:T(8,128)(2,1)} %bitcast.210), calls=%async_computation.1 | async-start | bytes 20971520 | tf_op jit(solution)/shard_map/all_to_all | solution.py:117
  57.7 2.1 pad_maximum_fusion
  72.9 2.4 convolution_bitcast_fusion
  82.7 2.4 convolution_bitcast_fusion.1
  85.3 5.2 %gather_fusion.1 = f32[32,5,128,128]{3,2,1,0:T(8,128)} fusion(f32[4,5,128,128]{3,2,1,0:T(8,128)S(1)} %copy.81, s32[1024]{0:T(1024)S(1)} %get-tuple-element.260), kind=kCustom, calls=%fused_computation.1.clone | custom fusion | bytes 20971648 | tf_op jit(solution)/shard_map/jit(_take)/gather | solution.py:85
  90.5 5.1 %gather_fusion = f32[32,5,128,128]{3,2,1,0:T(8,128)} fusion(f32[4,5,128,128]{3,2,1,0:T(8,128)S(1)} %copy.69, s32[1024]{0:T(1024)S(1)} %get-tuple-element.261), kind=kCustom, calls=%fused_computation.clone | custom fusion | bytes 20971648 | tf_op jit(solution)/shard_map/jit(_take)/gather | solution.py:85
  95.6 114.6 %all-to-all-done.1 = bf16[2,32,5,128,128]{4,3,2,0,1:T(8,128)(2,1)} async-done(((bf16[2,32,5,128,128]{4,3,2,0,1:T(8,128)(2,1)}), bf16[2,32,5,128,128]{4,3,2,0,1:T(8,128)(2,1)}, u32[]{:S(2)}, u32[]{:S(2)}) %all-to-all-start.1) | async-done | bytes 10485792 | tf_op jit(solution)/shard_map/all_to_all | solution.py:117
  210.2 15.5 %fusion.4 = (f32[32,5,128,128]{3,2,1,0:T(8,128)}, f32[32,5,128,128]{3,2,1,0:T(8,128)S(1)}) fusion(f32[32,5,128,128]{3,2,1,0:T(8,128)} %gather_fusion.1, bf16[2,32,5,128,128]{4,3,2,0,1:T(8,128)(2,1)} %all-to-all-done.1, f32[32]{0:T(128)S(1)} %get-tuple-element.6, pred[32]{0:T(512)(128)(4,1)S(1)} %get-tuple-element.14, f32[32,5,128,128]{3,2,1,0:T(8,128)} %gather_fusion, ...), kind=kLoop, calls=%fused_computation.7 | loop fusion | flops 20971520 | bytes 52429120 | tf_op jit(solution)/shard_map/mul | solution.py:86
  225.6 29.3 %fusion.15 = bf16[32,3,128,128]{3,1,2,0:T(4,128)(2,1)S(1)} fusion(f32[32,5,128,128]{3,2,1,0:T(8,128)S(1)} %get-tuple-element.38, f32[5,3]{0,1:T(4,128)S(1)} %copy-done.3), kind=kOutput, calls=%fused_computation.16 | convolution fusion | flops 95944704 | bytes 13631548 | tf_op jit(solution)/shard_map/hc,ohad->ocad/dot_general | solution.py:89
  254.9 3.4 %fusion.20 = f32[4,3,128,128]{3,0,2,1:T(4,128)S(1)} fusion(bf16[32,3,128,128]{3,1,2,0:T(4,128)(2,1)S(1)} %fusion.15, s32[32]{0:T(128)S(1)} %get-tuple-element.255, pred[32]{0:T(512)(128)(4,1)S(1)} %get-tuple-element.253), kind=kOutput, calls=%fused_computation.19 | convolution fusion | flops 12583168 | bytes 3932320 | tf_op jit(solution)/shard_map/ot,ocad->tcad/dot_general | solution.py:94
  261.0 10.7 %collective-permute-start.7 = (f32[3,12,256]{1,2,0:T(8,128)}, f32[3,12,256]{1,2,0:T(8,128)S(1)}, u32[]{:S(2)}, u32[]{:S(2)}) collective-permute-start(f32[3,12,256]{1,2,0:T(8,128)} %get-tuple-element.56), channel_id=1, source_target_pairs={{4,0},{8,4},{12,8},{16,12},{20,16},{24,20},{28,24},{32,28},{36,32}... | collective-permute-start | bytes 110600 | tf_op jit(solution)/shard_map/ppermute | solution.py:20
  271.7 5.9 %collective-permute-start.6 = (f32[3,12,256]{1,2,0:T(8,128)}, f32[3,12,256]{1,2,0:T(8,128)}, u32[]{:S(2)}, u32[]{:S(2)}) collective-permute-start(f32[3,12,256]{1,2,0:T(8,128)} %get-tuple-element.55), channel_id=1, source_target_pairs={{0,4},{4,8},{8,12},{12,16},{16,20},{20,24},{24,28},{28,32},{32,36}... | collective-permute-start | bytes 110600 | tf_op jit(solution)/shard_map/ppermute | solution.py:19
  277.6 25.1 %fusion.12 = bf16[32,3,128,128]{3,1,2,0:T(4,128)(2,1)S(1)} fusion(f32[32,5,128,128]{3,2,1,0:T(8,128)} %get-tuple-element.37, f32[5,3]{0,1:T(4,128)S(1)} %copy-done.3), kind=kOutput, calls=%fused_computation.15 | convolution fusion | flops 95944704 | bytes 13631548 | tf_op jit(solution)/shard_map/hc,ohad->ocad/dot_general | solution.py:89
  302.7 3.4 %fusion.18 = f32[4,3,128,128]{3,0,2,1:T(4,128)S(1)} fusion(bf16[32,3,128,128]{3,1,2,0:T(4,128)(2,1)S(1)} %fusion.12, s32[32]{0:T(128)S(1)} %get-tuple-element.254, pred[32]{0:T(512)(128)(4,1)S(1)} %get-tuple-element.252), kind=kOutput, calls=%fused_computation.17 | convolution fusion | flops 12583168 | bytes 3932320 | tf_op jit(solution)/shard_map/ot,ocad->tcad/dot_general | solution.py:94
  312.6 5.1 %collective-permute-start.8 = (f32[3,280,12]{1,2,0:T(8,128)S(1)}, f32[3,280,12]{1,2,0:T(8,128)S(1)}, u32[]{:S(2)}, u32[]{:S(2)}) collective-permute-start(f32[3,280,12]{1,2,0:T(8,128)S(1)} %get-tuple-element.47), channel_id=1, source_target_pairs={{0,1},{1,2},{2,3},{4,5},{5,6},{6,7},{8,9},{9,10},{10,11},{12,13},{... | collective-permute-start | bytes 120968 | tf_op jit(solution)/shard_map/ppermute | solution.py:28
  318.9 4.7 %collective-permute-done.10 = f32[3,12,256]{1,2,0:T(8,128)S(1)} collective-permute-done((f32[3,12,256]{1,2,0:T(8,128)S(1)}, f32[3,12,256]{1,2,0:T(8,128)S(1)}, u32[]{:S(2)}, u32[]{:S(2)}) %collective-permute-start.10) | collective-permute-done | bytes 36896 | tf_op jit(solution)/shard_map/ppermute | solution.py:19
  323.7 2.4 collective-permute-start.13
  326.1 4.7 %collective-permute-start.12 = (f32[3,280,12]{1,2,0:T(8,128)S(1)}, f32[3,280,12]{1,2,0:T(8,128)S(1)}, u32[]{:S(2)}, u32[]{:S(2)}) collective-permute-start(f32[3,280,12]{1,2,0:T(8,128)S(1)} %get-tuple-element.45), channel_id=1, source_target_pairs={{0,1},{1,2},{2,3},{4,5},{5,6},{6,7},{8,9},{9,10},{10,11},{12,13},{... | collective-permute-start | bytes 120968 | tf_op jit(solution)/shard_map/ppermute | solution.py:28
  (219 shorter events, 53.0 us)
Async XLA Ops:
  0.0 72.6 %copy-start = (bf16[128,128]{1,0:T(8,128)(2,1)S(1)}, bf16[128,128]{1,0:T(8,128)(2,1)}, u32[]{:S(2)}) copy-start(bf16[128,128]{1,0:T(8,128)(2,1)} %param.13) | copy-start | bytes 98308
  0.0 27.6 %copy-start.1 = (f32[3,256,256]{2,1,0:T(8,128)S(1)}, f32[3,256,256]{2,1,0:T(8,128)}, u32[]{:S(2)}) copy-start(f32[3,256,256]{2,1,0:T(8,128)} %param.10) | copy-start | bytes 2359300
  0.0 11.7 %copy-start.5 = (f32[256]{0:T(256)S(1)}, f32[256]{0:T(256)}, u32[]{:S(2)}) copy-start(f32[256]{0:T(256)} %param.12) | copy-start | bytes 3076
  0.0 19.7 %copy-start.6 = (bf16[2,1,1,32]{3,0,2,1:T(2,128)(2,1)S(1)}, bf16[2,1,1,32]{3,0,2,1:T(2,128)(2,1)}, u32[]{:S(2)}) copy-start(bf16[2,1,1,32]{3,0,2,1:T(2,128)(2,1)} %param.17) | copy-start | bytes 388
  0.0 27.5 %copy-start.4 = (s32[2,1,1,32]{3,2,1,0:T(1,128)S(1)}, s32[2,1,1,32]{3,2,1,0:T(1,128)}, u32[]{:S(2)}) copy-start(s32[2,1,1,32]{3,2,1,0:T(1,128)} %param.15) | copy-start | bytes 772
  4.6 37.1 %collective-permute-start.1 = (f32[4,12,256]{1,0,2:T(4,128)}, f32[4,12,256]{1,0,2:T(4,128)S(1)}, u32[]{:S(2)}, u32[]{:S(2)}) collective-permute-start(f32[4,12,256]{1,0,2:T(4,128)} %get-tuple-element.50), channel_id=1, source_target_pairs={{4,0},{8,4},{12,8},{16,12},{20,16},{24,20},{28,24},{32,28},{36,32}... | collective-permute-start | bytes 147464 | tf_op jit(solution)/shard_map/ppermute | solution.py:20
  11.7 30.0 %collective-permute-start = (f32[4,12,256]{1,0,2:T(4,128)}, f32[4,12,256]{1,0,2:T(4,128)S(1)}, u32[]{:S(2)}, u32[]{:S(2)}) collective-permute-start(f32[4,12,256]{1,0,2:T(4,128)} %get-tuple-element.49), channel_id=1, source_target_pairs={{0,4},{4,8},{8,12},{12,16},{16,20},{20,24},{24,28},{28,32},{32,36}... | collective-permute-start | bytes 147464 | tf_op jit(solution)/shard_map/ppermute | solution.py:19
  11.8 29.8 %collective-permute-start.5 = (f32[1,12]{1,0:T(1,128)S(1)}, f32[1,12]{1,0:T(1,128)S(1)}, u32[]{:S(2)}, u32[]{:S(2)}) collective-permute-start(f32[1,12]{1,0:T(1,128)S(1)} %get-tuple-element.259), channel_id=1, source_target_pairs={{1,0},{2,1},{3,2},{5,4},{6,5},{7,6},{9,8},{10,9},{11,10},{13,12},{... | collective-permute-start | bytes 152 | tf_op jit(solution)/shard_map/ppermute | solution.py:29
  14.6 26.9 %collective-permute-start.4 = (f32[1,12]{1,0:T(1,128)S(1)}, f32[1,12]{1,0:T(1,128)S(1)}, u32[]{:S(2)}, u32[]{:S(2)}) collective-permute-start(f32[1,12]{1,0:T(1,128)S(1)} %get-tuple-element.258), channel_id=1, source_target_pairs={{0,1},{1,2},{2,3},{4,5},{5,6},{6,7},{8,9},{9,10},{10,11},{12,13},{... | collective-permute-start | bytes 152 | tf_op jit(solution)/shard_map/ppermute | solution.py:28
  20.4 28.6 %all-to-all-start = ((bf16[2,32,1]{0,2,1:T(2,128)(2,1)}), bf16[2,32,1]{0,2,1:T(2,128)(2,1)S(1)}, u32[]{:S(2)}, u32[]{:S(2)}) async-start(bf16[2,32,1]{0,2,1:T(2,128)(2,1)} %copy.58), calls=%async_computation | async-start | bytes 32768 | tf_op jit(solution)/shard_map/all_to_all | solution.py:119
  41.9 15.7 %collective-permute-start.3 = (f32[4,280,12]{1,0,2:T(4,128)S(1)}, f32[4,280,12]{1,0,2:T(4,128)S(1)}, u32[]{:S(2)}, u32[]{:S(2)}) collective-permute-start(f32[4,280,12]{1,0,2:T(4,128)S(1)} %get-tuple-element.40), channel_id=1, source_target_pairs={{1,0},{2,1},{3,2},{5,4},{6,5},{7,6},{9,8},{10,9},{11,10},{13,12},{... | collective-permute-start | bytes 161288 | tf_op jit(solution)/shard_map/ppermute | solution.py:29
  43.9 13.8 %collective-permute-start.2 = (f32[4,280,12]{1,0,2:T(4,128)S(1)}, f32[4,280,12]{1,0,2:T(4,128)S(1)}, u32[]{:S(2)}, u32[]{:S(2)}) collective-permute-start(f32[4,280,12]{1,0,2:T(4,128)S(1)} %get-tuple-element.39), channel_id=1, source_target_pairs={{0,1},{1,2},{2,3},{4,5},{5,6},{6,7},{8,9},{9,10},{10,11},{12,13},{... | collective-permute-start | bytes 161288 | tf_op jit(solution)/shard_map/ppermute | solution.py:28
  49.0 161.1 %all-to-all-start.1 = ((bf16[2,32,5,128,128]{4,3,2,0,1:T(8,128)(2,1)}), bf16[2,32,5,128,128]{4,3,2,0,1:T(8,128)(2,1)}, u32[]{:S(2)}, u32[]{:S(2)}) async-start(bf16[2,32,5,128,128]{4,3,2,0,1:T(8,128)(2,1)} %bitcast.210), calls=%async_computation.1 | async-start | bytes 20971520 | tf_op jit(solution)/shard_map/all_to_all | solution.py:117
  70.4 2.5 copy-start.3
  261.0 48.7 %collective-permute-start.7 = (f32[3,12,256]{1,2,0:T(8,128)}, f32[3,12,256]{1,2,0:T(8,128)S(1)}, u32[]{:S(2)}, u32[]{:S(2)}) collective-permute-start(f32[3,12,256]{1,2,0:T(8,128)} %get-tuple-element.56), channel_id=1, source_target_pairs={{4,0},{8,4},{12,8},{16,12},{20,16},{24,20},{28,24},{32,28},{36,32}... | collective-permute-start | bytes 110600 | tf_op jit(solution)/shard_map/ppermute | solution.py:20
  271.7 38.1 %collective-permute-start.6 = (f32[3,12,256]{1,2,0:T(8,128)}, f32[3,12,256]{1,2,0:T(8,128)}, u32[]{:S(2)}, u32[]{:S(2)}) collective-permute-start(f32[3,12,256]{1,2,0:T(8,128)} %get-tuple-element.55), channel_id=1, source_target_pairs={{0,4},{4,8},{8,12},{12,16},{16,20},{20,24},{24,28},{28,32},{32,36}... | collective-permute-start | bytes 110600 | tf_op jit(solution)/shard_map/ppermute | solution.py:19
  308.2 10.7 %collective-permute-start.11 = (f32[3,12,256]{1,2,0:T(8,128)S(1)}, f32[3,12,256]{1,2,0:T(8,128)S(1)}, u32[]{:S(2)}, u32[]{:S(2)}) collective-permute-start(f32[3,12,256]{1,2,0:T(8,128)S(1)} %get-tuple-element.54), channel_id=1, source_target_pairs={{4,0},{8,4},{12,8},{16,12},{20,16},{24,20},{28,24},{32,28},{36,32}... | collective-permute-start | bytes 110600 | tf_op jit(solution)/shard_map/ppermute | solution.py:20
  308.2 15.3 %collective-permute-start.10 = (f32[3,12,256]{1,2,0:T(8,128)S(1)}, f32[3,12,256]{1,2,0:T(8,128)S(1)}, u32[]{:S(2)}, u32[]{:S(2)}) collective-permute-start(f32[3,12,256]{1,2,0:T(8,128)S(1)} %get-tuple-element.53), channel_id=1, source_target_pairs={{0,4},{4,8},{8,12},{12,16},{16,20},{20,24},{24,28},{28,32},{32,36}... | collective-permute-start | bytes 110600 | tf_op jit(solution)/shard_map/ppermute | solution.py:19
  310.7 20.1 %collective-permute-start.9 = (f32[3,280,12]{1,2,0:T(8,128)S(1)}, f32[3,280,12]{1,2,0:T(8,128)S(1)}, u32[]{:S(2)}, u32[]{:S(2)}) collective-permute-start(f32[3,280,12]{1,2,0:T(8,128)S(1)} %get-tuple-element.48), channel_id=1, source_target_pairs={{1,0},{2,1},{3,2},{5,4},{6,5},{7,6},{9,8},{10,9},{11,10},{13,12},{... | collective-permute-start | bytes 120968 | tf_op jit(solution)/shard_map/ppermute | solution.py:29
  312.6 18.2 %collective-permute-start.8 = (f32[3,280,12]{1,2,0:T(8,128)S(1)}, f32[3,280,12]{1,2,0:T(8,128)S(1)}, u32[]{:S(2)}, u32[]{:S(2)}) collective-permute-start(f32[3,280,12]{1,2,0:T(8,128)S(1)} %get-tuple-element.47), channel_id=1, source_target_pairs={{0,1},{1,2},{2,3},{4,5},{5,6},{6,7},{8,9},{9,10},{10,11},{12,13},{... | collective-permute-start | bytes 120968 | tf_op jit(solution)/shard_map/ppermute | solution.py:28
  323.7 13.0 %collective-permute-start.13 = (f32[3,280,12]{1,2,0:T(8,128)S(1)}, f32[3,280,12]{1,2,0:T(8,128)S(1)}, u32[]{:S(2)}, u32[]{:S(2)}) collective-permute-start(f32[3,280,12]{1,2,0:T(8,128)S(1)} %get-tuple-element.46), channel_id=1, source_target_pairs={{1,0},{2,1},{3,2},{5,4},{6,5},{7,6},{9,8},{10,9},{11,10},{13,12},{... | collective-permute-start | bytes 120968 | tf_op jit(solution)/shard_map/ppermute | solution.py:29
  326.1 10.6 %collective-permute-start.12 = (f32[3,280,12]{1,2,0:T(8,128)S(1)}, f32[3,280,12]{1,2,0:T(8,128)S(1)}, u32[]{:S(2)}, u32[]{:S(2)}) collective-permute-start(f32[3,280,12]{1,2,0:T(8,128)S(1)} %get-tuple-element.45), channel_id=1, source_target_pairs={{0,1},{1,2},{2,3},{4,5},{5,6},{6,7},{8,9},{9,10},{10,11},{12,13},{... | collective-permute-start | bytes 120968 | tf_op jit(solution)/shard_map/ppermute | solution.py:28
  341.8 1.1 copy-start.2
